TPU v7x, 256 devices: a whole 4x4x8 slice. The times are simulated.
256 devices in a mesh: dp: 16 (over x, y_hi, core), seq: 16 (over z, y_lo).
Axes of the slice: x: 4, y: 4 (y_hi: 2, y_lo: 2; y = y_hi * 2 + y_lo), z: 8, core: 2. Of those that a mesh axis runs over, the one named last changes fastest.
Arguments:
- queries: bfloat16 [40960, 768], P(('dp', 'seq')), may hold values from -8 to 8
- keys: bfloat16 [40960, 768], P(('dp', 'seq')), may hold values from -8 to 8
- values: bfloat16 [40960, 768], P(('dp', 'seq')), may hold values from -6 to 6
- frames: bfloat16 [40960, 768], P(('dp', 'seq')), may hold values from -4 to 4
- upstream: bfloat16 [40960, 768], P(('dp', 'seq')), may hold values from -6 to 6
- lengths: int32 [16], P('dp'), may hold values from 640 to 2560, as said below
- conv_kernel: bfloat16 [32, 768], replicated, may hold values from -1 to 1
Outputs:
- out: bfloat16 [40960, 768], P(('dp', 'seq'))
- query_grad: bfloat16 [40960, 768], P(('dp', 'seq'))
- key_grad: bfloat16 [40960, 768], P(('dp', 'seq'))
- value_grad: bfloat16 [40960, 768], P(('dp', 'seq'))
- frame_grad: bfloat16 [40960, 768], P(('dp', 'seq'))
- kernel_grad: float32 [32, 768], replicated
Inputs may be any that keep to these rules, and one draw needn't show every extreme that they name: `lengths`: one utterance has all 2560 frames live and another has 640.
All inputs are finite; a program needn't handle non-finite values.
Results may differ from a plain program's by a relative error of at most 0.0262.
Values may be sent and summed in bfloat16 or wider, within the bound.
No kernel may reach another device: no remote copies, remote signals or barrier semaphores. Data moves between devices by JAX's collectives and lax.ppermute only.
A program may use at most 128 MiB of HBM per device.

v0:
```python
import jax
import jax.numpy as jnp
from jax import lax
from jax.sharding import Mesh
from jax.sharding import PartitionSpec as P

HEAD_DIM = 64
KERNEL = 32
GROUPS = 4


def shifted(x, axis, by):
    count = lax.axis_size(axis)
    pairs = [(i, i + by) for i in range(count) if 0 <= i + by < count]
    return lax.ppermute(x, axis, pairs)


def butterfly_sum(x, axes):
    for axis in axes:
        count = lax.axis_size(axis)
        step = 1
        while step < count:
            x = x + lax.ppermute(x, axis, [(i, i ^ step) for i in range(count)])
            step = step * 2
    return x


def per_device(queries, keys, values, frames, upstream, lengths, conv_kernel):
    rows = queries.shape[0]
    channels = queries.shape[1]
    sub_count = lax.axis_size("sb")
    block_count_a = lax.axis_size("sa")
    group = channels // sub_count
    head_count = group // HEAD_DIM
    row_count = rows * sub_count
    span = row_count * block_count_a
    block_index = lax.axis_index("sa")
    group_index = lax.axis_index("sb")
    first_row = block_index * row_count
    length = lengths[0]
    score_scale = HEAD_DIM ** (-0.5)
    stacked = jnp.stack([queries, keys, values, frames, upstream])
    mixed = lax.all_to_all(
        stacked.reshape(5, rows, sub_count, group), "sb", 2, 1, tiled=True
    ).reshape(5, row_count, group)
    queries_b = mixed[0]
    frames_b = mixed[3]
    upstream_b = mixed[4]
    kv_all = lax.all_gather(jnp.concatenate([mixed[1], mixed[2]], axis=1), "sa", axis=0, tiled=True)
    key_all = kv_all[:, :group]
    value_all = kv_all[:, group:]
    key_block = row_count
    block_count = span // key_block
    key_blocks = key_all.reshape(block_count, key_block, head_count, HEAD_DIM)
    value_blocks = value_all.reshape(block_count, key_block, head_count, HEAD_DIM)
    block_starts = jnp.arange(block_count, dtype=jnp.int32) * key_block
    query_heads = queries_b.reshape(row_count, head_count, HEAD_DIM)

    def block_scores(key_part, block_start):
        scores = (
            jnp.einsum("thd,khd->htk", query_heads, key_part, preferred_element_type=jnp.float32)
            * score_scale
        )
        key_live = block_start + jnp.arange(key_part.shape[0], dtype=jnp.int32) < length
        return jnp.where(key_live[None, None, :], scores, -jnp.inf)

    def running_total(state_pair, block_items):
        running_top, total_sum = state_pair
        key_part, block_start = block_items
        scores = block_scores(key_part, block_start)
        higher = jnp.maximum(running_top, jnp.max(scores, axis=2))
        total_sum = total_sum * jnp.exp(running_top - higher) + jnp.sum(
            jnp.exp(scores - higher[:, :, None]), axis=2
        )
        return ((higher, total_sum), None)

    start_state = (
        jnp.full((head_count, row_count), -1e30, jnp.float32),
        jnp.zeros((head_count, row_count), jnp.float32),
    )
    (running_top, total_sum), unused = lax.scan(
        running_total, start_state, (key_blocks, block_starts)
    )
    log_total = running_top + jnp.log(total_sum)

    def attend_block(attend_acc, block_items):
        key_part, value_part, block_start = block_items
        prob_bf = jnp.exp(block_scores(key_part, block_start) - log_total[:, :, None]).astype(
            jnp.bfloat16
        )
        return (
            attend_acc
            + jnp.einsum("htk,khd->thd", prob_bf, value_part, preferred_element_type=jnp.float32),
            None,
        )

    attend_acc, unused = lax.scan(
        attend_block,
        jnp.zeros((row_count, head_count, HEAD_DIM), jnp.float32),
        (key_blocks, value_blocks, block_starts),
    )
    attended = attend_acc.reshape(row_count, group).astype(jnp.bfloat16)
    frame_live = (first_row + jnp.arange(row_count, dtype=jnp.int32) < length)[:, None]
    hidden = (frames_b.astype(jnp.float32) + attended.astype(jnp.float32)).astype(jnp.bfloat16)
    masked = jnp.where(frame_live, hidden, jnp.zeros_like(hidden))
    past_rows = shifted(masked[row_count - (KERNEL - 1) :], "sa", 1)
    extended = jnp.concatenate([past_rows, masked], axis=0).astype(jnp.float32)
    weights = lax.dynamic_slice_in_dim(conv_kernel, group_index * group, group, axis=1).astype(
        jnp.float32
    )
    conv_out = jnp.zeros((row_count, group), jnp.float32)
    for tap_index in range(KERNEL):
        conv_out = (
            conv_out
            + weights[tap_index]
            * extended[KERNEL - 1 - tap_index : KERNEL - 1 - tap_index + row_count]
        )
    sig_conv = jax.nn.sigmoid(conv_out)
    out = (hidden.astype(jnp.float32) + conv_out * sig_conv).astype(jnp.bfloat16)
    loss_grad = jnp.where(frame_live, upstream_b.astype(jnp.float32), 0.0)
    conv_grad = (loss_grad * sig_conv * (1.0 + conv_out * (1.0 - sig_conv))).astype(jnp.bfloat16)
    conv_float = conv_grad.astype(jnp.float32)
    kernel_part = jnp.stack(
        [
            jnp.sum(
                conv_float * extended[KERNEL - 1 - tap_index : KERNEL - 1 - tap_index + row_count],
                axis=0,
            )
            for tap_index in range(KERNEL)
        ]
    )
    future_rows = shifted(conv_grad[: KERNEL - 1], "sa", -1)
    ahead_rows = jnp.concatenate([conv_grad, future_rows], axis=0).astype(jnp.float32)
    back_conv = jnp.zeros((row_count, group), jnp.float32)
    for tap_index in range(KERNEL):
        back_conv = back_conv + weights[tap_index] * ahead_rows[tap_index : tap_index + row_count]
    frame_grad = (loss_grad + jnp.where(frame_live, back_conv, 0.0)).astype(jnp.bfloat16)
    grad_heads = frame_grad.reshape(row_count, head_count, HEAD_DIM)
    attended_heads = attended.reshape(row_count, head_count, HEAD_DIM)
    delta_rows = jnp.sum(
        grad_heads.astype(jnp.float32) * attended_heads.astype(jnp.float32), axis=2
    ).T

    def score_grads(key_part, value_part, block_start):
        soft_weights = jnp.exp(block_scores(key_part, block_start) - log_total[:, :, None])
        prob_grad = jnp.einsum(
            "thd,khd->htk", grad_heads, value_part, preferred_element_type=jnp.float32
        )
        score_grad = (soft_weights * (prob_grad - delta_rows[:, :, None])).astype(jnp.bfloat16)
        return (soft_weights.astype(jnp.bfloat16), score_grad)

    def gradient_block(query_acc, block_items):
        key_part, value_part, block_start = block_items
        prob_bf, score_grad = score_grads(key_part, value_part, block_start)
        query_acc = query_acc + jnp.einsum(
            "htk,khd->thd", score_grad, key_part, preferred_element_type=jnp.float32
        )
        key_term = (
            jnp.einsum("htk,thd->khd", score_grad, query_heads, preferred_element_type=jnp.float32)
            * score_scale
        )
        value_term = jnp.einsum(
            "htk,thd->khd", prob_bf, grad_heads, preferred_element_type=jnp.float32
        )
        grad_terms = jnp.concatenate(
            [key_term.reshape(key_block, group), value_term.reshape(key_block, group)], axis=1
        )
        return (query_acc, grad_terms)

    query_acc, grad_terms = lax.scan(
        gradient_block,
        jnp.zeros((row_count, head_count, HEAD_DIM), jnp.float32),
        (key_blocks, value_blocks, block_starts),
    )
    own_rows = lax.psum_scatter(
        grad_terms.reshape(span, 2 * group).astype(jnp.bfloat16),
        "sa",
        scatter_dimension=0,
        tiled=True,
    ).astype(jnp.float32)
    key_grad = own_rows[:, :group].astype(jnp.bfloat16)
    value_grad = own_rows[:, group:].astype(jnp.bfloat16)
    query_grad = (query_acc * score_scale).reshape(row_count, group).astype(jnp.bfloat16)
    kernel_full = lax.dynamic_update_slice_in_dim(
        jnp.zeros((KERNEL, channels), jnp.float32), kernel_part, group_index * group, axis=1
    )
    kernel_total = butterfly_sum(kernel_full, ("sb", "sa", "dp"))
    kernel_grad = kernel_total / lax.axis_size("dp")
    results = jnp.stack([out, query_grad, key_grad, value_grad, frame_grad])
    spread = lax.all_to_all(
        results.reshape(5, sub_count, rows, 1, group), "sb", 1, 3, tiled=True
    ).reshape(5, rows, channels)
    return (spread[0], spread[1], spread[2], spread[3], spread[4], kernel_grad)


def solution(mesh):
    seq_count = mesh.shape["seq"]
    split_mesh = Mesh(
        mesh.devices.reshape(mesh.shape["dp"], seq_count // GROUPS, GROUPS), ("dp", "sa", "sb")
    )
    rows_spec = P(("dp", "sa", "sb"), None)
    placed = (rows_spec, rows_spec, rows_spec, rows_spec, rows_spec, P("dp"), P())
    return jax.shard_map(
        per_device,
        mesh=split_mesh,
        in_specs=placed,
        out_specs=(rows_spec, rows_spec, rows_spec, rows_spec, rows_spec, P()),
        check_vma=False,
    )
```

profile of v0, /device:TPU:2, one launch (start us, length us, event | category | flops | bytes accessed | tf_op | source)
XLA Modules:
  0.0 392.6 jit_solution(232273346341479808)
XLA Ops:
  12.7 24.6 %all_to_all.30 = bf16[5,160,4,192]{3,1,0,2:T(8,128)(2,1)S(1)} all-to-all(bf16[5,160,4,192]{3,1,0,2:T(8,128)(2,1)S(1)} %copy.80), channel_id=1, replica_groups=mesh['dp'=16,'sa'=4,'sb'=4] {'sb'}, dimensions={2} | all-to-all | bytes 2457600 | tf_op jit(solution)/shard_map/all_to_all | solution.py:43
  41.8 47.3 %all-gather.2.cloned.1.call-done = bf16[2560,384]{1,0:T(8,128)(2,1)} async-done(((bf16[640,384]{1,0:T(8,128)(2,1)}), bf16[2560,384]{1,0:T(8,128)(2,1)}) %all-gather.2.cloned.1.call-update) | async-done | bytes 1966096 | tf_op jit(solution)/shard_map/all_gather | solution.py:49
  89.1 2.3 fusion.111
  95.8 40.8 %while.37 = (s32[]{:T(128)}, f32[3,640]{1,0:T(4,128)S(1)}, f32[3,640]{1,0:T(4,128)S(1)}, s32[4]{0:T(128)}, s32[]{:T(128)}, /*index=5*/bf16[4,640,3,64]{1,3,2,0:T...) while((s32[]{:T(128)}, f32[3,640]{1,0:T(4,128)S(1)}, f32[3,640]{1,0:T(4,128)S(1)}, ...), condition=%wide.region_3.4_spmd.clone, body=%wide.region_0.3_spmd.clone.sunk | while | flops 165898880 | bytes 10424316 | solution.py:81
  98.4 4.1 %bitcast_reduce_fusion.2 = (f32[3,640]{1,0:T(4,128)S(1)}, f32[3,640,640]{2,1,0:T(8,128)}) fusion(pred[640]{0:T(1024)(128)(4,1)S(1)} %add_compare_fusion.7, bf16[640,3,64]{0,2,1:T(8,128)(2,1)S(1)} %get-tuple-element.670, bf16[4,640,3,64]{1,3,2,0:T(8,128)(2,1)} %get-tuple-element.669, s32[]{:T(128)} %get-tuple-element.655), kind=kOutput, calls=%fused_computation.1.clone.1 | convolution fusion | flops 160970880 | bytes 5415552 | tf_op jit(solution)/shard_map/while/body/eval_jaxpr/thd,khd->htk/dot_general | solution.py:61
  102.5 3.4 fusion.146
  108.6 4.1 %bitcast_reduce_fusion.2 = (f32[3,640]{1,0:T(4,128)S(1)}, f32[3,640,640]{2,1,0:T(8,128)}) fusion(pred[640]{0:T(1024)(128)(4,1)S(1)} %add_compare_fusion.7, bf16[640,3,64]{0,2,1:T(8,128)(2,1)S(1)} %get-tuple-element.670, bf16[4,640,3,64]{1,3,2,0:T(8,128)(2,1)} %get-tuple-element.669, s32[]{:T(128)} %get-tuple-element.655), kind=kOutput, calls=%fused_computation.1.clone.1 | convolution fusion | flops 160970880 | bytes 5415552 | tf_op jit(solution)/shard_map/while/body/eval_jaxpr/thd,khd->htk/dot_general | solution.py:61
  112.7 3.4 fusion.146
  118.8 4.1 %bitcast_reduce_fusion.2 = (f32[3,640]{1,0:T(4,128)S(1)}, f32[3,640,640]{2,1,0:T(8,128)}) fusion(pred[640]{0:T(1024)(128)(4,1)S(1)} %add_compare_fusion.7, bf16[640,3,64]{0,2,1:T(8,128)(2,1)S(1)} %get-tuple-element.670, bf16[4,640,3,64]{1,3,2,0:T(8,128)(2,1)} %get-tuple-element.669, s32[]{:T(128)} %get-tuple-element.655), kind=kOutput, calls=%fused_computation.1.clone.1 | convolution fusion | flops 160970880 | bytes 5415552 | tf_op jit(solution)/shard_map/while/body/eval_jaxpr/thd,khd->htk/dot_general | solution.py:61
  123.0 3.4 fusion.146
  129.0 4.1 %bitcast_reduce_fusion.2 = (f32[3,640]{1,0:T(4,128)S(1)}, f32[3,640,640]{2,1,0:T(8,128)}) fusion(pred[640]{0:T(1024)(128)(4,1)S(1)} %add_compare_fusion.7, bf16[640,3,64]{0,2,1:T(8,128)(2,1)S(1)} %get-tuple-element.670, bf16[4,640,3,64]{1,3,2,0:T(8,128)(2,1)} %get-tuple-element.669, s32[]{:T(128)} %get-tuple-element.655), kind=kOutput, calls=%fused_computation.1.clone.1 | convolution fusion | flops 160970880 | bytes 5415552 | tf_op jit(solution)/shard_map/while/body/eval_jaxpr/thd,khd->htk/dot_general | solution.py:61
  133.2 3.4 fusion.146
  138.2 24.5 %while.38 = (s32[]{:T(128)}, f32[640,3,64]{0,2,1:T(8,128)}, bf16[4,640,3,64]{1,3,2,0:T(8,128)(2,1)S(1)}, s32[4]{0:T(128)}, s32[]{:T(128)}, /*index=5*/bf16[4,640...) while((s32[]{:T(128)}, f32[640,3,64]{0,2,1:T(8,128)}, ...), condition=%wide.region_5.6_spmd.clone, body=%wide.region_4.5_spmd.clone.sunk | while | flops 319735040 | bytes 1733379 | solution.py:97
  140.8 3.4 fusion.151
  146.8 3.6 fusion.151
  152.9 3.6 fusion.151
  159.1 3.6 fusion.151
  165.3 5.2 %collective-permute-start = (bf16[31,192]{1,0:T(8,128)(2,1)S(1)}, bf16[31,192]{1,0:T(8,128)(2,1)S(1)}, u32[]{:S(2)}, u32[]{:S(2)}) collective-permute-start(bf16[31,192]{1,0:T(8,128)(2,1)S(1)} %slice.531), channel_id=1, source_target_pairs={{0,4},{4,8},{8,12},{1,5},{5,9},{9,13},{2,6},{6,10},{10,14},{3,7},{... | collective-permute-start | bytes 35720 | tf_op jit(solution)/shard_map/ppermute | solution.py:15
  172.1 7.1 %fusion.71 = (f32[192]{0:T(256)}, f32[192]{0:T(256)}, f32[192]{0:T(256)}, f32[192]{0:T(256)}, f32[192]{0:T(256)}, /*index=5*/f32[192]{0:T(256)}, f32[192]{0:T(25...) fusion(f32[671,192]{1,0:T(8,128)S(1)} %maximum_convert_fusion, ...), kind=kLoop, calls=%fused_computation.113 | loop fusion | flops 13636224 | bytes 16750720 | tf_op jit(solution)/shard_map/reduce_sum | solution.py:125
  180.5 5.6 %collective-permute-done.1 = bf16[31,192]{1,0:T(8,128)(2,1)S(1)} collective-permute-done((bf16[31,192]{1,0:T(8,128)(2,1)S(1)}, bf16[31,192]{1,0:T(8,128)(2,1)S(1)}, u32[]{:S(2)}, u32[]{:S(2)}) %collective-permute-start.1) | collective-permute-done | bytes 11936 | tf_op jit(solution)/shard_map/ppermute | solution.py:15
  186.2 3.1 fusion.75
  191.2 70.0 %while.39 = (s32[]{:T(128)}, f32[640,3,64]{0,2,1:T(8,128)}, bf16[4,640,384]{2,1,0:T(8,128)(2,1)}, bf16[4,640,3,64]{1,3,2,0:T(8,128)(2,1)}, s32[4]{0:T(128)}, /*i...) while((s32[]{:T(128)}, f32[640,3,64]{0,2,1:T(8,128)}, ...), condition=%wide.region_8.9_spmd.clone, body=%wide.region_7.8_spmd.clone.sunk | while | flops 800195840 | bytes 28292124 | solution.py:170
  195.7 2.7 multiply_convert_fusion.3
  199.3 2.3 fusion.164
  206.3 2.3 fusion.163
  213.0 2.7 multiply_convert_fusion.3
  216.6 2.3 fusion.164
  223.6 2.5 fusion.163
  230.6 2.7 multiply_convert_fusion.3
  234.2 2.3 fusion.164
  241.2 2.5 fusion.163
  248.1 2.7 multiply_convert_fusion.3
  251.7 2.3 fusion.164
  258.7 2.5 fusion.163
  261.2 2.9 fusion.70
  264.8 44.9 %reduce-scatter.2.cloned.1.call-done = bf16[640,384]{1,0:T(8,128)(2,1)} async-done(((bf16[2560,384]{1,0:T(8,128)(2,1)}), bf16[640,384]{1,0:T(8,128)(2,1)}) %reduce-scatter.2.cloned.1.call-update) | async-done | bytes 491536 | tf_op jit(solution)/shard_map/reduce_scatter | solution.py:175
  312.4 3.6 all-to-all-start.1
  316.8 2.4 collective-permute-start.2
  319.2 19.0 %collective-permute-done.2 = f32[32,768]{1,0:T(8,128)S(1)} collective-permute-done((f32[32,768]{1,0:T(8,128)S(1)}, f32[32,768]{1,0:T(8,128)S(1)}, u32[]{:S(2)}, u32[]{:S(2)}) %collective-permute-start.2) | collective-permute-done | bytes 98336 | tf_op jit(solution)/shard_map/ppermute | solution.py:23
  340.2 3.2 collective-permute-done.3
  343.5 2.5 collective-permute-start.4
  345.9 4.4 %collective-permute-done.4 = f32[32,768]{1,0:T(8,128)S(1)} collective-permute-done((f32[32,768]{1,0:T(8,128)S(1)}, f32[32,768]{1,0:T(8,128)S(1)}, u32[]{:S(2)}, u32[]{:S(2)}) %collective-permute-start.4) | collective-permute-done | bytes 98336 | tf_op jit(solution)/shard_map/ppermute | solution.py:23
  350.3 2.5 collective-permute-start.5
  352.8 7.1 %collective-permute-done.5 = f32[32,768]{1,0:T(8,128)S(1)} collective-permute-done((f32[32,768]{1,0:T(8,128)S(1)}, f32[32,768]{1,0:T(8,128)S(1)}, u32[]{:S(2)}, u32[]{:S(2)}) %collective-permute-start.5) | collective-permute-done | bytes 98336 | tf_op jit(solution)/shard_map/ppermute | solution.py:23
  361.3 3.2 collective-permute-start.7
  364.5 3.3 collective-permute-done.7
  368.3 4.2 %collective-permute-done.8 = f32[32,768]{1,0:T(8,128)S(1)} collective-permute-done((f32[32,768]{1,0:T(8,128)S(1)}, f32[32,768]{1,0:T(8,128)S(1)}, u32[]{:S(2)}, u32[]{:S(2)}) %collective-permute-start.8) | collective-permute-done | bytes 98336 | tf_op jit(solution)/shard_map/ppermute | solution.py:23
  374.7 4.0 %collective-permute-done.9 = f32[32,768]{1,0:T(8,128)S(1)} collective-permute-done((f32[32,768]{1,0:T(8,128)S(1)}, f32[32,768]{1,0:T(8,128)S(1)}, u32[]{:S(2)}, u32[]{:S(2)}) %collective-permute-start.9) | collective-permute-done | bytes 98336 | tf_op jit(solution)/shard_map/ppermute | solution.py:23
  (236 shorter events, 100.1 us)
Async XLA Ops:
  7.2 4.1 %copy-start.8 = (bf16[160,768]{1,0:T(8,128)(2,1)S(1)}, bf16[160,768]{1,0:T(8,128)(2,1)}, u32[]{:S(2)}) copy-start(bf16[160,768]{1,0:T(8,128)(2,1)} %param.16) | copy-start | bytes 737284
  7.2 4.4 %copy-start.9 = (bf16[160,768]{1,0:T(8,128)(2,1)S(1)}, bf16[160,768]{1,0:T(8,128)(2,1)}, u32[]{:S(2)}) copy-start(bf16[160,768]{1,0:T(8,128)(2,1)} %param.17) | copy-start | bytes 737284
  7.2 81.9 %all-gather.2.cloned.1.call-start = ((), (), s32[]{:S(2)}) async-start(), calls=%async_computation.3 | async-start | bytes 2457600 | tf_op jit(solution)/shard_map/all_gather | solution.py:49
  37.4 127.7 %copy-start.3 = (bf16[1,4,160,1,192]{4,2,0,1,3:T(8,128)(2,1)}, bf16[1,4,160,1,192]{4,2,0,1,3:T(8,128)(2,1)S(1)}, u32[]{:S(2)}) copy-start(bf16[1,4,160,1,192]{4,2,0,1,3:T(8,128)(2,1)S(1)} %get-tuple-element.447) | copy-start | bytes 737284
  38.5 271.2 %reduce-scatter.2.cloned.1.call-start = ((), (), s32[]{:S(2)}) async-start(), calls=%async_computation.4 | async-start | bytes 2457600 | tf_op jit(solution)/shard_map/reduce_scatter | solution.py:175
  163.7 8.2 %copy-start.11 = (f32[1,192]{1,0:T(1,128)S(1)}, f32[1,192]{1,0:T(1,128)}, u32[]{:S(2)}) copy-start(f32[1,192]{1,0:T(1,128)} %get-tuple-element.451) | copy-start | bytes 2308
  163.7 8.2 %copy-start.12 = (f32[1,192]{1,0:T(1,128)S(1)}, f32[1,192]{1,0:T(1,128)}, u32[]{:S(2)}) copy-start(f32[1,192]{1,0:T(1,128)} %get-tuple-element.452) | copy-start | bytes 2308
  163.7 8.3 %copy-start.13 = (f32[1,192]{1,0:T(1,128)S(1)}, f32[1,192]{1,0:T(1,128)}, u32[]{:S(2)}) copy-start(f32[1,192]{1,0:T(1,128)} %get-tuple-element.453) | copy-start | bytes 2308
  163.7 8.3 %copy-start.14 = (f32[1,192]{1,0:T(1,128)S(1)}, f32[1,192]{1,0:T(1,128)}, u32[]{:S(2)}) copy-start(f32[1,192]{1,0:T(1,128)} %get-tuple-element.454) | copy-start | bytes 2308
  163.7 8.3 %copy-start.15 = (f32[1,192]{1,0:T(1,128)S(1)}, f32[1,192]{1,0:T(1,128)}, u32[]{:S(2)}) copy-start(f32[1,192]{1,0:T(1,128)} %get-tuple-element.455) | copy-start | bytes 2308
  163.7 8.3 %copy-start.16 = (f32[1,192]{1,0:T(1,128)S(1)}, f32[1,192]{1,0:T(1,128)}, u32[]{:S(2)}) copy-start(f32[1,192]{1,0:T(1,128)} %get-tuple-element.456) | copy-start | bytes 2308
  163.7 8.3 %copy-start.17 = (f32[1,192]{1,0:T(1,128)S(1)}, f32[1,192]{1,0:T(1,128)}, u32[]{:S(2)}) copy-start(f32[1,192]{1,0:T(1,128)} %get-tuple-element.457) | copy-start | bytes 2308
  163.7 8.3 %copy-start.18 = (f32[1,192]{1,0:T(1,128)S(1)}, f32[1,192]{1,0:T(1,128)}, u32[]{:S(2)}) copy-start(f32[1,192]{1,0:T(1,128)} %get-tuple-element.458) | copy-start | bytes 2308
  163.7 8.3 %copy-start.19 = (f32[1,192]{1,0:T(1,128)S(1)}, f32[1,192]{1,0:T(1,128)}, u32[]{:S(2)}) copy-start(f32[1,192]{1,0:T(1,128)} %get-tuple-element.459) | copy-start | bytes 2308
  163.7 8.3 %copy-start.20 = (f32[1,192]{1,0:T(1,128)S(1)}, f32[1,192]{1,0:T(1,128)}, u32[]{:S(2)}) copy-start(f32[1,192]{1,0:T(1,128)} %get-tuple-element.460) | copy-start | bytes 2308
  163.7 8.3 %copy-start.21 = (f32[1,192]{1,0:T(1,128)S(1)}, f32[1,192]{1,0:T(1,128)}, u32[]{:S(2)}) copy-start(f32[1,192]{1,0:T(1,128)} %get-tuple-element.461) | copy-start | bytes 2308
  163.8 8.3 %copy-start.22 = (f32[1,192]{1,0:T(1,128)S(1)}, f32[1,192]{1,0:T(1,128)}, u32[]{:S(2)}) copy-start(f32[1,192]{1,0:T(1,128)} %get-tuple-element.462) | copy-start | bytes 2308
  163.8 8.3 %copy-start.23 = (f32[1,192]{1,0:T(1,128)S(1)}, f32[1,192]{1,0:T(1,128)}, u32[]{:S(2)}) copy-start(f32[1,192]{1,0:T(1,128)} %get-tuple-element.463) | copy-start | bytes 2308
  163.8 8.3 %copy-start.24 = (f32[1,192]{1,0:T(1,128)S(1)}, f32[1,192]{1,0:T(1,128)}, u32[]{:S(2)}) copy-start(f32[1,192]{1,0:T(1,128)} %get-tuple-element.464) | copy-start | bytes 2308
  163.8 8.3 %copy-start.25 = (f32[1,192]{1,0:T(1,128)S(1)}, f32[1,192]{1,0:T(1,128)}, u32[]{:S(2)}) copy-start(f32[1,192]{1,0:T(1,128)} %get-tuple-element.465) | copy-start | bytes 2308
  163.8 8.3 %copy-start.26 = (f32[1,192]{1,0:T(1,128)S(1)}, f32[1,192]{1,0:T(1,128)}, u32[]{:S(2)}) copy-start(f32[1,192]{1,0:T(1,128)} %get-tuple-element.466) | copy-start | bytes 2308
  163.8 8.3 %copy-start.27 = (f32[1,192]{1,0:T(1,128)S(1)}, f32[1,192]{1,0:T(1,128)}, u32[]{:S(2)}) copy-start(f32[1,192]{1,0:T(1,128)} %get-tuple-element.467) | copy-start | bytes 2308
  163.8 8.3 %copy-start.28 = (f32[1,192]{1,0:T(1,128)S(1)}, f32[1,192]{1,0:T(1,128)}, u32[]{:S(2)}) copy-start(f32[1,192]{1,0:T(1,128)} %get-tuple-element.468) | copy-start | bytes 2308
  165.1 6.4 %copy-start.1 = (f32[640,192]{1,0:T(8,128)}, f32[640,192]{1,0:T(8,128)S(1)}, u32[]{:S(2)}) copy-start(f32[640,192]{1,0:T(8,128)S(1)} %copy.87) | copy-start | bytes 1474564
  165.3 6.5 %collective-permute-start = (bf16[31,192]{1,0:T(8,128)(2,1)S(1)}, bf16[31,192]{1,0:T(8,128)(2,1)S(1)}, u32[]{:S(2)}, u32[]{:S(2)}) collective-permute-start(bf16[31,192]{1,0:T(8,128)(2,1)S(1)} %slice.531), channel_id=1, source_target_pairs={{0,4},{4,8},{8,12},{1,5},{5,9},{9,13},{2,6},{6,10},{10,14},{3,7},{... | collective-permute-start | bytes 35720 | tf_op jit(solution)/shard_map/ppermute | solution.py:15
  179.2 10.2 %copy-start.2 = (bf16[640,192]{1,0:T(8,128)(2,1)}, bf16[640,192]{1,0:T(8,128)(2,1)S(1)}, u32[]{:S(2)}) copy-start(bf16[640,192]{1,0:T(8,128)(2,1)S(1)} %get-tuple-element.432) | copy-start | bytes 737284
  179.2 6.9 %collective-permute-start.1 = (bf16[31,192]{1,0:T(8,128)(2,1)S(1)}, bf16[31,192]{1,0:T(8,128)(2,1)S(1)}, u32[]{:S(2)}, u32[]{:S(2)}) collective-permute-start(bf16[31,192]{1,0:T(8,128)(2,1)S(1)} %slice.596), channel_id=1, source_target_pairs={{4,0},{8,4},{12,8},{5,1},{9,5},{13,9},{6,2},{10,6},{14,10},{7,3},{... | collective-permute-start | bytes 35720 | tf_op jit(solution)/shard_map/ppermute | solution.py:15
  186.2 4.0 %copy-start.6 = (f32[640,3,64]{0,2,1:T(8,128)S(1)}, f32[640,3,64]{0,2,1:T(8,128)}, u32[]{:S(2)}) copy-start(f32[640,3,64]{0,2,1:T(8,128)} %get-tuple-element.146) | copy-start | bytes 1474564
  264.2 46.8 %copy-start.5 = (bf16[640,192]{1,0:T(8,128)(2,1)S(1)}, bf16[640,192]{1,0:T(8,128)(2,1)}, u32[]{:S(2)}) copy-start(bf16[640,192]{1,0:T(8,128)(2,1)} %copy-done.4) | copy-start | bytes 737284
  312.3 3.8 copy-start.33
  312.3 3.8 copy-start.34
  312.3 3.8 copy-start.35
  312.3 3.8 copy-start.36
  312.3 3.8 copy-start.37
  312.3 3.8 copy-start.38
  312.4 3.8 copy-start.39
  312.4 3.8 copy-start.40
  312.4 3.8 copy-start.41
  312.4 3.8 copy-start.42
  312.4 66.9 %all-to-all-start.1 = ((bf16[5,4,160,1,192]{4,2,3,0,1:T(8,128)(2,1)}), bf16[5,4,160,1,192]{4,2,3,0,1:T(8,128)(2,1)S(1)}, u32[]{:S(2)}, u32[]{:S(2)}) async-start(bf16[5,4,160,1,192]{4,2,3,0,1:T(8,128)(2,1)} %copy.93), calls=%async_computation.2 | async-start | bytes 3276800 | tf_op jit(solution)/shard_map/all_to_all | solution.py:190
  316.8 21.4 %collective-permute-start.2 = (f32[32,768]{1,0:T(8,128)S(1)}, f32[32,768]{1,0:T(8,128)S(1)}, u32[]{:S(2)}, u32[]{:S(2)}) collective-permute-start(f32[32,768]{1,0:T(8,128)S(1)} %dynamic_update_slice.9), channel_id=1, source_target_pairs={{0,1},{1,0},{2,3},{3,2},{4,5},{5,4},{6,7},{7,6},{8,9},{9,8},{10,11... | collective-permute-start | bytes 294920 | tf_op jit(solution)/shard_map/ppermute | solution.py:23
  338.7 4.7 %collective-permute-start.3 = (f32[32,768]{1,0:T(8,128)S(1)}, f32[32,768]{1,0:T(8,128)S(1)}, u32[]{:S(2)}, u32[]{:S(2)}) collective-permute-start(f32[32,768]{1,0:T(8,128)S(1)} %add.364), channel_id=1, source_target_pairs={{0,2},{1,3},{2,0},{3,1},{4,6},{5,7},{6,4},{7,5},{8,10},{9,11},{10,... | collective-permute-start | bytes 294920 | tf_op jit(solution)/shard_map/ppermute | solution.py:23
  343.5 6.8 %collective-permute-start.4 = (f32[32,768]{1,0:T(8,128)S(1)}, f32[32,768]{1,0:T(8,128)S(1)}, u32[]{:S(2)}, u32[]{:S(2)}) collective-permute-start(f32[32,768]{1,0:T(8,128)S(1)} %add.365), channel_id=1, source_target_pairs={{0,4},{4,0},{8,12},{12,8},{1,5},{5,1},{9,13},{13,9},{2,6},{6,2},{1... | collective-permute-start | bytes 294920 | tf_op jit(solution)/shard_map/ppermute | solution.py:23
  350.3 9.6 %collective-permute-start.5 = (f32[32,768]{1,0:T(8,128)S(1)}, f32[32,768]{1,0:T(8,128)S(1)}, u32[]{:S(2)}, u32[]{:S(2)}) collective-permute-start(f32[32,768]{1,0:T(8,128)S(1)} %add.366), channel_id=1, source_target_pairs={{0,8},{4,12},{8,0},{12,4},{1,9},{5,13},{9,1},{13,5},{2,10},{6,14},... | collective-permute-start | bytes 294920 | tf_op jit(solution)/shard_map/ppermute | solution.py:23
  359.9 1.4 collective-permute-start.6
  361.3 6.4 %collective-permute-start.7 = (f32[32,768]{1,0:T(8,128)S(1)}, f32[32,768]{1,0:T(8,128)S(1)}, u32[]{:S(2)}, u32[]{:S(2)}) collective-permute-start(f32[32,768]{1,0:T(8,128)S(1)} %add.368), channel_id=1, source_target_pairs={{0,32},{16,48},{32,0},{48,16},{64,96},{80,112},{96,64},{112,80},{1... | collective-permute-start | bytes 294920 | tf_op jit(solution)/shard_map/ppermute | solution.py:23
  367.8 4.7 %collective-permute-start.8 = (f32[32,768]{1,0:T(8,128)S(1)}, f32[32,768]{1,0:T(8,128)S(1)}, u32[]{:S(2)}, u32[]{:S(2)}) collective-permute-start(f32[32,768]{1,0:T(8,128)S(1)} %add.369), channel_id=1, source_target_pairs={{0,64},{16,80},{32,96},{48,112},{64,0},{80,16},{96,32},{112,48},{1... | collective-permute-start | bytes 294920 | tf_op jit(solution)/shard_map/ppermute | solution.py:23
  372.5 6.2 %collective-permute-start.9 = (f32[32,768]{1,0:T(8,128)S(1)}, f32[32,768]{1,0:T(8,128)S(1)}, u32[]{:S(2)}, u32[]{:S(2)}) collective-permute-start(f32[32,768]{1,0:T(8,128)S(1)} %add.370), channel_id=1, source_target_pairs={{0,128},{16,144},{32,160},{48,176},{64,192},{80,208},{96,224},{112... | collective-permute-start | bytes 294920 | tf_op jit(solution)/shard_map/ppermute | solution.py:23
  (12 other events, 37.0 us)
Sparse Core Ops, SparseCore 0:
  38.6 50.4 all-gather.1
  261.3 48.2 reduce-scatter.1
where the time goes:
time: 395 us; the launch traced here: 393 us
  waiting for transfers between devices  145 us (37%)
  matrix products  71.1 us (18%)
  local copies, waits for them, and re-layouts  59.1 us (15%)
  other arithmetic  52.1 us (13%)
  starting transfers between devices  25 us (6%)
  blocking collectives  24.6 us (6%)
  between operations  15.7 us (4%)
    all_gather x1, waiting for transfers between devices, per_device(): lax.all_gather(jnp.concatenate([mixed[1], mixed[2]], axis=1), 'sa', axis=...  47.3 us
    ppermute x8, waiting for transfers between devices, butterfly_sum(): x = x + lax.ppermute(x, axis, [(i, i ^ step) for i in range(count)])  46.5 us
    reduce_scatter x1, waiting for transfers between devices, per_device(): lax.psum_scatter(grad_terms.reshape(span, 2 * group).astype(jnp.bfloat16)...  44.9 us
    all_to_all x1, blocking collectives, per_device(): lax.all_to_all(stacked.reshape(5, rows, sub_count, group), 'sb', 2, 1, ti...  24.6 us
    dot_general x8, matrix products, block_scores(): jnp.einsum('thd,khd->htk', query_heads, key_part, preferred_element_type=...  23.7 us
    lt x12, other arithmetic, block_scores(): block_start + jnp.arange(key_part.shape[0], dtype=jnp.int32) < length  15.6 us
    dynamic_slice x12, local copies, waits for them, and re-layouts, per_device(): lax.scan(running_total, start_state, (key_blocks, block_starts))  15.6 us
    dynamic_update_slice x8, local copies, waits for them, and re-layouts, per_device(): lax.scan(gradient_block, jnp.zeros((row_count, head_count, HEAD_DIM), jnp...  15.5 us
  transfers between devices with their start and end apart: 13, of which 12 were waited for; matrix products, arithmetic and copies ran while one was open for 2% of the time, Pallas kernels for 0%

commit v1 on v0

--- a/solution.py
+++ b/solution.py
@@ -40,8 +40,16 @@
     length = lengths[0]
     score_scale = HEAD_DIM ** (-0.5)
     stacked = jnp.stack([queries, keys, values, frames, upstream])
-    mixed = lax.all_to_all(
-        stacked.reshape(5, rows, sub_count, group), "sb", 2, 1, tiled=True
+    mixed = jnp.concatenate(
+        lax.all_to_all(
+            jnp.stack(
+                jnp.split(stacked.reshape(5, rows, sub_count, group), lax.axis_size("sb"), axis=2)
+            ),
+            "sb",
+            0,
+            0,
+        ),
+        axis=1,
     ).reshape(5, row_count, group)
     queries_b = mixed[0]
     frames_b = mixed[3]

time: 395 us -> 346 us (0.88)
  matrix products: 71.1 us -> 44.1 us
  other arithmetic: 52.1 us -> 37.4 us
  local copies, waits for them, and re-layouts: 59.1 us -> 53.8 us
    dot_general x8, matrix products: 23.7 us -> 7.51 us  [block_scores(): jnp.einsum('thd,khd->htk', query_heads, key_part, preferred_element_type=...]
    dynamic_update_slice x8, local copies, waits for them, and re-layouts: 15.5 us -> 4.42 us  [per_device(): lax.scan(gradient_block, jnp.zeros((row_count, head_count, HEAD_DIM), jnp...]
    reduce_sum x4, other arithmetic: 13.8 us -> 4.17 us  [running_total(): jnp.sum(jnp.exp(scores - higher[:, :, None]), axis=2)]
    dot_general x4, matrix products: 9.72 us -> 2.36 us  [gradient_block(): jnp.einsum('htk,khd->thd', score_grad, key_part, preferred_element_type=j...]
    dynamic_slice x12, local copies, waits for them, and re-layouts: 15.6 us -> 10 us  [per_device(): lax.scan(running_total, start_state, (key_blocks, block_starts))]
  transfers between devices with their start and end apart: 13 -> 13, of which waited for: 12 -> 12; matrix products, arithmetic and copies ran while one was open for 2% -> 3% of each run, Pallas kernels for 0% -> 0%
where the time goes in v1:
time: 346 us; the launch traced here: 345 us
  waiting for transfers between devices  143 us (41%)
  local copies, waits for them, and re-layouts  53.8 us (16%)
  matrix products  44.1 us (13%)
  other arithmetic  37.4 us (11%)
  starting transfers between devices  24.9 us (7%)
  blocking collectives  24.6 us (7%)
  between operations  15.8 us (5%)
    all_gather x1, waiting for transfers between devices, per_device(): lax.all_gather(jnp.concatenate([mixed[1], mixed[2]], axis=1), 'sa', axis=...  47.3 us
    ppermute x8, waiting for transfers between devices, butterfly_sum(): x = x + lax.ppermute(x, axis, [(i, i ^ step) for i in range(count)])  45.5 us
    reduce_scatter x1, waiting for transfers between devices, per_device(): lax.psum_scatter(grad_terms.reshape(span, 2 * group).astype(jnp.bfloat16)...  44.7 us
    all_to_all x1, blocking collectives, per_device(): lax.all_to_all(jnp.stack(jnp.split(stacked.reshape(5, rows, sub_count, gr...  24.6 us
    lt x12, other arithmetic, block_scores(): block_start + jnp.arange(key_part.shape[0], dtype=jnp.int32) < length  15.4 us
    ppermute x8, starting transfers between devices, butterfly_sum(): x = x + lax.ppermute(x, axis, [(i, i ^ step) for i in range(count)])  14.4 us
    dot_general x4, matrix products, score_grads(): jnp.einsum('thd,khd->htk', grad_heads, value_part, preferred_element_type...  10.8 us
    dot_general x4, matrix products, attend_block(): jnp.einsum('htk,khd->thd', prob_bf, value_part, preferred_element_type=jn...  10.8 us
  transfers between devices with their start and end apart: 13, of which 12 were waited for; matrix products, arithmetic and copies ran while one was open for 3% of the time, Pallas kernels for 0%

profile of v1, /device:TPU:2, one launch (start us, length us, event | category | flops | bytes accessed | tf_op | source)
XLA Modules:
  0.0 344.6 jit_solution(11747614028367697863)
XLA Ops:
  7.2 1.3 stack.148
  13.3 3.3 fusion.114
  17.4 24.6 %all_to_all.20 = bf16[4,5,160,1,192]{4,2,1,3,0:T(8,128)(2,1)S(1)} all-to-all(bf16[4,5,160,1,192]{4,2,1,3,0:T(8,128)(2,1)S(1)} %pad_maximum_fusion), channel_id=1, replica_groups=mesh['dp'=16,'sa'=4,'sb'=4] {'sb'}, dimensions={0} | all-to-all | bytes 2457600 | tf_op jit(solution)/shard_map/all_to_all | solution.py:44
  47.3 47.3 %all-gather.2.cloned.1.call-done = bf16[2560,384]{1,0:T(8,128)(2,1)} async-done(((bf16[640,384]{1,0:T(8,128)(2,1)}), bf16[2560,384]{1,0:T(8,128)(2,1)}) %all-gather.2.cloned.1.call-update) | async-done | bytes 1966096 | tf_op jit(solution)/shard_map/all_gather | solution.py:57
  94.7 3.4 fusion.111
  98.1 1.6 copy.110
  100.0 18.6 %while.37 = (s32[]{:T(128)}, f32[3,640]{1,0:T(4,128)S(1)}, f32[3,640]{1,0:T(4,128)S(1)}, s32[4]{0:T(128)}, s32[]{:T(128)}, /*index=5*/bf16[4,640,3,64]{1,3,2,0:T...) while((s32[]{:T(128)}, f32[3,640]{1,0:T(4,128)S(1)}, f32[3,640]{1,0:T(4,128)S(1)}, ...), condition=%wide.region_3.4_spmd.clone, body=%wide.region_0.3_spmd.clone.sunk | while | flops 165898880 | bytes 10424200 | solution.py:89
  120.6 18.8 %while.38 = (s32[]{:T(128)}, f32[640,3,64]{0,2,1:T(8,128)S(1)}, bf16[4,640,3,64]{1,3,2,0:T(8,128)(2,1)}, s32[4]{0:T(128)S(1)}, s32[]{:T(128)}, /*index=5*/bf16[4...) while((s32[]{:T(128)}, f32[640,3,64]{0,2,1:T(8,128)S(1)}, ...), condition=%wide.region_5.6_spmd.clone, body=%wide.region_4.5_spmd.clone.sunk | while | flops 319735040 | bytes 1733898 | solution.py:105
  121.2 1.3 add_compare_fusion.8
  122.6 2.7 fusion.152
  125.9 1.3 add_compare_fusion.8
  127.3 2.7 fusion.152
  130.6 1.3 add_compare_fusion.8
  132.0 2.7 fusion.152
  135.3 1.3 add_compare_fusion.8
  136.7 2.7 fusion.152
  140.4 1.3 copy.115
  141.9 5.3 %collective-permute-start = (bf16[31,192]{1,0:T(8,128)(2,1)S(1)}, bf16[31,192]{1,0:T(8,128)(2,1)S(1)}, u32[]{:S(2)}, u32[]{:S(2)}) collective-permute-start(bf16[31,192]{1,0:T(8,128)(2,1)S(1)} %slice.531), channel_id=1, source_target_pairs={{0,4},{4,8},{8,12},{1,5},{5,9},{9,13},{2,6},{6,10},{10,14},{3,7},{... | collective-permute-start | bytes 35720 | tf_op jit(solution)/shard_map/ppermute | solution.py:15
  148.7 7.1 %fusion.71 = (f32[192]{0:T(256)}, f32[192]{0:T(256)}, f32[192]{0:T(256)}, f32[192]{0:T(256)}, f32[192]{0:T(256)}, /*index=5*/f32[192]{0:T(256)}, f32[192]{0:T(25...) fusion(f32[671,192]{1,0:T(8,128)S(1)} %maximum_convert_fusion, ...), kind=kLoop, calls=%fused_computation.114 | loop fusion | flops 13636224 | bytes 16750720 | tf_op jit(solution)/shard_map/reduce_sum | solution.py:133
  155.8 1.3 collective-permute-start.1
  157.1 5.6 %collective-permute-done.1 = bf16[31,192]{1,0:T(8,128)(2,1)S(1)} collective-permute-done((bf16[31,192]{1,0:T(8,128)(2,1)S(1)}, bf16[31,192]{1,0:T(8,128)(2,1)S(1)}, u32[]{:S(2)}, u32[]{:S(2)}) %collective-permute-start.1) | collective-permute-done | bytes 11936 | tf_op jit(solution)/shard_map/ppermute | solution.py:15
  162.8 3.1 fusion.75
  168.1 41.5 %while.39 = (s32[]{:T(128)}, f32[640,3,64]{0,2,1:T(8,128)S(1)}, bf16[4,640,384]{2,1,0:T(8,128)(2,1)}, bf16[4,640,3,64]{1,3,2,0:T(8,128)(2,1)S(1)}, s32[4]{0:T(12...) while((s32[]{:T(128)}, f32[640,3,64]{0,2,1:T(8,128)S(1)}, ...), condition=%wide.region_8.9_spmd.clone, body=%wide.region_7.8_spmd.clone.sunk | while | flops 800195840 | bytes 28287540 | solution.py:178
  170.9 2.3 fusion.165
  173.1 2.7 multiply_convert_fusion.3
  181.2 2.3 fusion.165
  183.5 2.7 multiply_convert_fusion.3
  191.6 2.2 fusion.165
  193.9 2.7 multiply_convert_fusion.3
  202.0 2.3 fusion.165
  204.2 2.7 multiply_convert_fusion.3
  213.4 44.7 %reduce-scatter.2.cloned.1.call-done = bf16[640,384]{1,0:T(8,128)(2,1)} async-done(((bf16[2560,384]{1,0:T(8,128)(2,1)}), bf16[640,384]{1,0:T(8,128)(2,1)}) %reduce-scatter.2.cloned.1.call-update) | async-done | bytes 491536 | tf_op jit(solution)/shard_map/reduce_scatter | solution.py:183
  261.5 2.7 copy.121
  264.3 3.9 %all-to-all-start.1 = ((bf16[5,4,160,1,192]{4,2,3,0,1:T(8,128)(2,1)}), bf16[5,4,160,1,192]{4,2,3,0,1:T(8,128)(2,1)S(1)}, u32[]{:S(2)}, u32[]{:S(2)}) async-start(bf16[5,4,160,1,192]{4,2,3,0,1:T(8,128)(2,1)} %copy.121), calls=%async_computation.2 | async-start | bytes 3276800 | tf_op jit(solution)/shard_map/all_to_all | solution.py:198
  270.3 2.0 collective-permute-start.2
  272.2 17.9 %collective-permute-done.2 = f32[32,768]{1,0:T(8,128)S(1)} collective-permute-done((f32[32,768]{1,0:T(8,128)S(1)}, f32[32,768]{1,0:T(8,128)S(1)}, u32[]{:S(2)}, u32[]{:S(2)}) %collective-permute-start.2) | collective-permute-done | bytes 98336 | tf_op jit(solution)/shard_map/ppermute | solution.py:23
  290.7 1.5 collective-permute-start.3
  292.2 3.2 collective-permute-done.3
  295.4 2.5 collective-permute-start.4
  297.9 4.4 %collective-permute-done.4 = f32[32,768]{1,0:T(8,128)S(1)} collective-permute-done((f32[32,768]{1,0:T(8,128)S(1)}, f32[32,768]{1,0:T(8,128)S(1)}, u32[]{:S(2)}, u32[]{:S(2)}) %collective-permute-start.4) | collective-permute-done | bytes 98336 | tf_op jit(solution)/shard_map/ppermute | solution.py:23
  302.3 2.6 collective-permute-start.5
  304.9 7.1 %collective-permute-done.5 = f32[32,768]{1,0:T(8,128)S(1)} collective-permute-done((f32[32,768]{1,0:T(8,128)S(1)}, f32[32,768]{1,0:T(8,128)S(1)}, u32[]{:S(2)}, u32[]{:S(2)}) %collective-permute-start.5) | collective-permute-done | bytes 98336 | tf_op jit(solution)/shard_map/ppermute | solution.py:23
  312.1 1.3 collective-permute-done.6
  313.4 3.1 collective-permute-start.7
  316.5 3.4 collective-permute-done.7
  320.5 4.1 %collective-permute-done.8 = f32[32,768]{1,0:T(8,128)S(1)} collective-permute-done((f32[32,768]{1,0:T(8,128)S(1)}, f32[32,768]{1,0:T(8,128)S(1)}, u32[]{:S(2)}, u32[]{:S(2)}) %collective-permute-start.8) | collective-permute-done | bytes 98336 | tf_op jit(solution)/shard_map/ppermute | solution.py:23
  324.6 2.1 collective-permute-start.9
  326.6 4.1 %collective-permute-done.9 = f32[32,768]{1,0:T(8,128)S(1)} collective-permute-done((f32[32,768]{1,0:T(8,128)S(1)}, f32[32,768]{1,0:T(8,128)S(1)}, u32[]{:S(2)}, u32[]{:S(2)}) %collective-permute-start.9) | collective-permute-done | bytes 98336 | tf_op jit(solution)/shard_map/ppermute | solution.py:23
  (250 shorter events, 76.7 us)
Async XLA Ops:
  7.2 5.1 %copy-start.12 = (bf16[160,768]{1,0:T(8,128)(2,1)S(1)}, bf16[160,768]{1,0:T(8,128)(2,1)}, u32[]{:S(2)}) copy-start(bf16[160,768]{1,0:T(8,128)(2,1)} %param.17) | copy-start | bytes 737284
  7.2 87.5 %all-gather.2.cloned.1.call-start = ((), (), s32[]{:S(2)}) async-start(), calls=%async_computation.3 | async-start | bytes 2457600 | tf_op jit(solution)/shard_map/all_gather | solution.py:57
  44.1 214.0 %reduce-scatter.2.cloned.1.call-start = ((), (), s32[]{:S(2)}) async-start(), calls=%async_computation.4 | async-start | bytes 2457600 | tf_op jit(solution)/shard_map/reduce_scatter | solution.py:183
  46.1 51.9 %copy-start.13 = (f32[32,192]{1,0:T(8,128)}, f32[32,192]{1,0:T(8,128)S(1)}, u32[]{:S(2)}) copy-start(f32[32,192]{1,0:T(8,128)S(1)} %dynamic-slice_convert_fusion) | copy-start | bytes 73732
  139.4 9.1 %copy-start.11 = (f32[640,3,64]{0,2,1:T(8,128)}, f32[640,3,64]{0,2,1:T(8,128)S(1)}, u32[]{:S(2)}) copy-start(f32[640,3,64]{0,2,1:T(8,128)S(1)} %get-tuple-element.146) | copy-start | bytes 1474564
  139.4 2.3 copy-start.4
  140.2 8.3 %copy-start.8 = (bf16[1,4,160,1,192]{4,2,0,3,1:T(8,128)(2,1)S(1)}, bf16[1,4,160,1,192]{4,2,0,3,1:T(8,128)(2,1)}, u32[]{:S(2)}) copy-start(bf16[1,4,160,1,192]{4,2,0,3,1:T(8,128)(2,1)} %get-tuple-element.495) | copy-start | bytes 737284
  140.2 8.3 %copy-start.14 = (f32[1,192]{1,0:T(1,128)S(1)}, f32[1,192]{1,0:T(1,128)}, u32[]{:S(2)}) copy-start(f32[1,192]{1,0:T(1,128)} %get-tuple-element.507) | copy-start | bytes 2308
  140.2 8.3 %copy-start.15 = (f32[1,192]{1,0:T(1,128)S(1)}, f32[1,192]{1,0:T(1,128)}, u32[]{:S(2)}) copy-start(f32[1,192]{1,0:T(1,128)} %get-tuple-element.508) | copy-start | bytes 2308
  140.2 8.3 %copy-start.16 = (f32[1,192]{1,0:T(1,128)S(1)}, f32[1,192]{1,0:T(1,128)}, u32[]{:S(2)}) copy-start(f32[1,192]{1,0:T(1,128)} %get-tuple-element.509) | copy-start | bytes 2308
  140.2 8.3 %copy-start.17 = (f32[1,192]{1,0:T(1,128)S(1)}, f32[1,192]{1,0:T(1,128)}, u32[]{:S(2)}) copy-start(f32[1,192]{1,0:T(1,128)} %get-tuple-element.510) | copy-start | bytes 2308
  140.3 8.3 %copy-start.18 = (f32[1,192]{1,0:T(1,128)S(1)}, f32[1,192]{1,0:T(1,128)}, u32[]{:S(2)}) copy-start(f32[1,192]{1,0:T(1,128)} %get-tuple-element.511) | copy-start | bytes 2308
  140.3 8.3 %copy-start.19 = (f32[1,192]{1,0:T(1,128)S(1)}, f32[1,192]{1,0:T(1,128)}, u32[]{:S(2)}) copy-start(f32[1,192]{1,0:T(1,128)} %get-tuple-element.512) | copy-start | bytes 2308
  140.3 8.3 %copy-start.20 = (f32[1,192]{1,0:T(1,128)S(1)}, f32[1,192]{1,0:T(1,128)}, u32[]{:S(2)}) copy-start(f32[1,192]{1,0:T(1,128)} %get-tuple-element.513) | copy-start | bytes 2308
  140.3 8.3 %copy-start.21 = (f32[1,192]{1,0:T(1,128)S(1)}, f32[1,192]{1,0:T(1,128)}, u32[]{:S(2)}) copy-start(f32[1,192]{1,0:T(1,128)} %get-tuple-element.514) | copy-start | bytes 2308
  140.3 8.3 %copy-start.22 = (f32[1,192]{1,0:T(1,128)S(1)}, f32[1,192]{1,0:T(1,128)}, u32[]{:S(2)}) copy-start(f32[1,192]{1,0:T(1,128)} %get-tuple-element.515) | copy-start | bytes 2308
  140.3 8.3 %copy-start.23 = (f32[1,192]{1,0:T(1,128)S(1)}, f32[1,192]{1,0:T(1,128)}, u32[]{:S(2)}) copy-start(f32[1,192]{1,0:T(1,128)} %get-tuple-element.516) | copy-start | bytes 2308
  140.3 8.3 %copy-start.24 = (f32[1,192]{1,0:T(1,128)S(1)}, f32[1,192]{1,0:T(1,128)}, u32[]{:S(2)}) copy-start(f32[1,192]{1,0:T(1,128)} %get-tuple-element.517) | copy-start | bytes 2308
  140.3 8.3 %copy-start.25 = (f32[1,192]{1,0:T(1,128)S(1)}, f32[1,192]{1,0:T(1,128)}, u32[]{:S(2)}) copy-start(f32[1,192]{1,0:T(1,128)} %get-tuple-element.518) | copy-start | bytes 2308
  140.3 8.3 %copy-start.26 = (f32[1,192]{1,0:T(1,128)S(1)}, f32[1,192]{1,0:T(1,128)}, u32[]{:S(2)}) copy-start(f32[1,192]{1,0:T(1,128)} %get-tuple-element.519) | copy-start | bytes 2308
  140.3 8.3 %copy-start.27 = (f32[1,192]{1,0:T(1,128)S(1)}, f32[1,192]{1,0:T(1,128)}, u32[]{:S(2)}) copy-start(f32[1,192]{1,0:T(1,128)} %get-tuple-element.520) | copy-start | bytes 2308
  140.4 8.3 %copy-start.28 = (f32[1,192]{1,0:T(1,128)S(1)}, f32[1,192]{1,0:T(1,128)}, u32[]{:S(2)}) copy-start(f32[1,192]{1,0:T(1,128)} %get-tuple-element.521) | copy-start | bytes 2308
  140.4 8.3 %copy-start.29 = (f32[1,192]{1,0:T(1,128)S(1)}, f32[1,192]{1,0:T(1,128)}, u32[]{:S(2)}) copy-start(f32[1,192]{1,0:T(1,128)} %get-tuple-element.522) | copy-start | bytes 2308
  140.4 8.3 %copy-start.30 = (f32[1,192]{1,0:T(1,128)S(1)}, f32[1,192]{1,0:T(1,128)}, u32[]{:S(2)}) copy-start(f32[1,192]{1,0:T(1,128)} %get-tuple-element.523) | copy-start | bytes 2308
  140.4 8.3 %copy-start.31 = (f32[1,192]{1,0:T(1,128)S(1)}, f32[1,192]{1,0:T(1,128)}, u32[]{:S(2)}) copy-start(f32[1,192]{1,0:T(1,128)} %get-tuple-element.524) | copy-start | bytes 2308
  141.7 6.4 %copy-start = (f32[640,192]{1,0:T(8,128)}, f32[640,192]{1,0:T(8,128)S(1)}, u32[]{:S(2)}) copy-start(f32[640,192]{1,0:T(8,128)S(1)} %copy.115) | copy-start | bytes 1474564
  141.9 6.5 %collective-permute-start = (bf16[31,192]{1,0:T(8,128)(2,1)S(1)}, bf16[31,192]{1,0:T(8,128)(2,1)S(1)}, u32[]{:S(2)}, u32[]{:S(2)}) collective-permute-start(bf16[31,192]{1,0:T(8,128)(2,1)S(1)} %slice.531), channel_id=1, source_target_pairs={{0,4},{4,8},{8,12},{1,5},{5,9},{9,13},{2,6},{6,10},{10,14},{3,7},{... | collective-permute-start | bytes 35720 | tf_op jit(solution)/shard_map/ppermute | solution.py:15
  155.8 10.1 %copy-start.2 = (bf16[640,192]{1,0:T(8,128)(2,1)}, bf16[640,192]{1,0:T(8,128)(2,1)S(1)}, u32[]{:S(2)}) copy-start(bf16[640,192]{1,0:T(8,128)(2,1)S(1)} %get-tuple-element.484) | copy-start | bytes 737284
  155.8 6.9 %collective-permute-start.1 = (bf16[31,192]{1,0:T(8,128)(2,1)S(1)}, bf16[31,192]{1,0:T(8,128)(2,1)S(1)}, u32[]{:S(2)}, u32[]{:S(2)}) collective-permute-start(bf16[31,192]{1,0:T(8,128)(2,1)S(1)} %slice.596), channel_id=1, source_target_pairs={{4,0},{8,4},{12,8},{5,1},{9,5},{13,9},{6,2},{10,6},{14,10},{7,3},{... | collective-permute-start | bytes 35720 | tf_op jit(solution)/shard_map/ppermute | solution.py:15
  162.8 5.3 %copy-start.51 = (s32[4]{0:T(128)S(1)}, s32[4]{0:T(128)}, u32[]{:S(2)}) copy-start(s32[4]{0:T(128)} %get-tuple-element.838) | copy-start | bytes 52
  166.0 2.1 copy-start.6
  209.6 1.4 copy-start.9
  212.3 48.5 %copy-start.7 = (bf16[640,192]{1,0:T(8,128)(2,1)S(1)}, bf16[640,192]{1,0:T(8,128)(2,1)}, u32[]{:S(2)}) copy-start(bf16[640,192]{1,0:T(8,128)(2,1)} %copy-done.6) | copy-start | bytes 737284
  264.3 3.9 %copy-start.3 = (bf16[640,192]{1,0:T(8,128)(2,1)S(1)}, bf16[640,192]{1,0:T(8,128)(2,1)}, u32[]{:S(2)}) copy-start(bf16[640,192]{1,0:T(8,128)(2,1)} %copy-done.2) | copy-start | bytes 737284
  264.3 67.2 %all-to-all-start.1 = ((bf16[5,4,160,1,192]{4,2,3,0,1:T(8,128)(2,1)}), bf16[5,4,160,1,192]{4,2,3,0,1:T(8,128)(2,1)S(1)}, u32[]{:S(2)}, u32[]{:S(2)}) async-start(bf16[5,4,160,1,192]{4,2,3,0,1:T(8,128)(2,1)} %copy.121), calls=%async_computation.2 | async-start | bytes 3276800 | tf_op jit(solution)/shard_map/all_to_all | solution.py:198
  268.2 1.3 copy-start.32
  268.2 1.3 copy-start.33
  268.2 1.3 copy-start.34
  268.2 1.3 copy-start.35
  268.3 1.3 copy-start.36
  270.3 19.9 %collective-permute-start.2 = (f32[32,768]{1,0:T(8,128)S(1)}, f32[32,768]{1,0:T(8,128)S(1)}, u32[]{:S(2)}, u32[]{:S(2)}) collective-permute-start(f32[32,768]{1,0:T(8,128)S(1)} %dynamic_update_slice.9), channel_id=1, source_target_pairs={{0,1},{1,0},{2,3},{3,2},{4,5},{5,4},{6,7},{7,6},{8,9},{9,8},{10,11... | collective-permute-start | bytes 294920 | tf_op jit(solution)/shard_map/ppermute | solution.py:23
  290.7 4.7 %collective-permute-start.3 = (f32[32,768]{1,0:T(8,128)S(1)}, f32[32,768]{1,0:T(8,128)S(1)}, u32[]{:S(2)}, u32[]{:S(2)}) collective-permute-start(f32[32,768]{1,0:T(8,128)S(1)} %add.364), channel_id=1, source_target_pairs={{0,2},{1,3},{2,0},{3,1},{4,6},{5,7},{6,4},{7,5},{8,10},{9,11},{10,... | collective-permute-start | bytes 294920 | tf_op jit(solution)/shard_map/ppermute | solution.py:23
  295.4 6.8 %collective-permute-start.4 = (f32[32,768]{1,0:T(8,128)S(1)}, f32[32,768]{1,0:T(8,128)S(1)}, u32[]{:S(2)}, u32[]{:S(2)}) collective-permute-start(f32[32,768]{1,0:T(8,128)S(1)} %add.365), channel_id=1, source_target_pairs={{0,4},{4,0},{8,12},{12,8},{1,5},{5,1},{9,13},{13,9},{2,6},{6,2},{1... | collective-permute-start | bytes 294920 | tf_op jit(solution)/shard_map/ppermute | solution.py:23
  302.3 9.7 %collective-permute-start.5 = (f32[32,768]{1,0:T(8,128)S(1)}, f32[32,768]{1,0:T(8,128)S(1)}, u32[]{:S(2)}, u32[]{:S(2)}) collective-permute-start(f32[32,768]{1,0:T(8,128)S(1)} %add.366), channel_id=1, source_target_pairs={{0,8},{4,12},{8,0},{12,4},{1,9},{5,13},{9,1},{13,5},{2,10},{6,14},... | collective-permute-start | bytes 294920 | tf_op jit(solution)/shard_map/ppermute | solution.py:23
  312.0 1.4 collective-permute-start.6
  313.4 6.4 %collective-permute-start.7 = (f32[32,768]{1,0:T(8,128)S(1)}, f32[32,768]{1,0:T(8,128)S(1)}, u32[]{:S(2)}, u32[]{:S(2)}) collective-permute-start(f32[32,768]{1,0:T(8,128)S(1)} %add.368), channel_id=1, source_target_pairs={{0,32},{16,48},{32,0},{48,16},{64,96},{80,112},{96,64},{112,80},{1... | collective-permute-start | bytes 294920 | tf_op jit(solution)/shard_map/ppermute | solution.py:23
  319.8 4.7 %collective-permute-start.8 = (f32[32,768]{1,0:T(8,128)S(1)}, f32[32,768]{1,0:T(8,128)S(1)}, u32[]{:S(2)}, u32[]{:S(2)}) collective-permute-start(f32[32,768]{1,0:T(8,128)S(1)} %add.369), channel_id=1, source_target_pairs={{0,64},{16,80},{32,96},{48,112},{64,0},{80,16},{96,32},{112,48},{1... | collective-permute-start | bytes 294920 | tf_op jit(solution)/shard_map/ppermute | solution.py:23
  324.6 6.2 %collective-permute-start.9 = (f32[32,768]{1,0:T(8,128)S(1)}, f32[32,768]{1,0:T(8,128)S(1)}, u32[]{:S(2)}, u32[]{:S(2)}) collective-permute-start(f32[32,768]{1,0:T(8,128)S(1)} %add.370), channel_id=1, source_target_pairs={{0,128},{16,144},{32,160},{48,176},{64,192},{80,208},{96,224},{112... | collective-permute-start | bytes 294920 | tf_op jit(solution)/shard_map/ppermute | solution.py:23
  (17 other events, 21.4 us)
Sparse Core Ops, SparseCore 0:
  44.2 50.4 all-gather.1
  209.8 48.2 reduce-scatter.1
